TPU v7x, 32 devices: a whole 2x2x4 slice. The times are simulated.
32 devices in a mesh: groups: 2 (over y), tensor: 4 (over x, core), dp: 4 (over z).
Axes of the slice: x: 2, y: 2, z: 4, core: 2. Of those that a mesh axis runs over, the one named last changes fastest.
Arguments:
- tokens: bfloat16 [65536, 4096], P(('groups', 'dp'), 'tensor'), parts along dimension 0, may hold values from -6 to 6
- cotangent: bfloat16 [65536, 4096], P(('groups', 'dp'), 'tensor'), parts along dimension 0, may hold values from -6 to 6
- w_first: bfloat16 [16, 256, 256], P('tensor'), may hold values from -0.375 to 0.375
- w_second: bfloat16 [16, 256, 256], P('tensor'), may hold values from -0.375 to 0.375
Outputs:
- grad_tokens: bfloat16 [65536, 4096], P(('groups', 'dp'), 'tensor'), parts along dimension 0
- grad_first: float32 [32, 256, 256], P(('groups', 'tensor'), 'dp'), parts along dimension 0
- grad_second: float32 [32, 256, 256], P(('groups', 'tensor'), 'dp'), parts along dimension 0
There are 2 independent parts, one for each index of `groups`. A program takes and returns all parts, laid end to end along the dimension named above; an argument that names none is the same for every part. Nothing has to cross between parts.
All inputs are finite; a program needn't handle non-finite values.
Results may differ from a plain program's by a relative error of at most 0.0065.
Values may be sent and summed in bfloat16 or wider, within the bound.
No kernel may reach another device: no remote copies, remote signals or barrier semaphores. Data moves between devices by JAX's collectives and lax.ppermute only.
A program may use at most 192 MiB of HBM per device.

v0:
```python
import math
import jax
import jax.numpy as jnp
from jax import lax
from jax.sharding import PartitionSpec as P

NB = 16
CHUNKS = 4


def expanded_weights(w_first, w_second, n_dev):
    blk_local, bs, _ = w_first.shape
    sub = bs // NB
    eye = jnp.eye(blk_local, dtype=jnp.bool_)
    zero = jnp.zeros((), w_first.dtype)
    w1r = w_first.reshape(blk_local, bs, n_dev, blk_local, sub)
    w1p = jnp.where(eye[:, None, None, None, :, None], w1r[:, :, :, :, None, :], zero).reshape(
        blk_local * bs, blk_local * bs
    )
    w2r = w_second.reshape(blk_local, sub, n_dev, blk_local, bs).transpose(0, 4, 2, 3, 1)
    w2p = jnp.where(eye[:, None, None, :, None, None], w2r[:, :, :, None, :, :], zero).reshape(
        blk_local * bs, blk_local * bs
    )
    w1t = w_first.reshape(blk_local, bs, NB, sub).transpose(2, 3, 0, 1)
    w1tp = jnp.where(eye[None, :, None, :, None], w1t[:, None, :, :, :], zero).reshape(
        blk_local * bs, blk_local * bs
    )
    return (w1p, w2p, w1tp)


def shards(tokens, cotangent, w_first, w_second):
    tok_rows = tokens.shape[0]
    blk_local, bs, _ = w_first.shape
    feat = blk_local * bs
    sub = bs // NB
    n_dev = lax.axis_size("tensor")
    dp_count = lax.axis_size("dp")
    grad_scale = 1.0 / math.sqrt(tok_rows * dp_count)
    w1p, w2p, w1tp = expanded_weights(w_first, w_second, n_dev)
    step = tok_rows // CHUNKS
    gf_acc = None
    gs_acc = None
    outs = []
    for k in range(CHUNKS):
        x = tokens[k * step : (k + 1) * step]
        cot = cotangent[k * step : (k + 1) * step]
        hidden = jnp.dot(x, w1p, preferred_element_type=jnp.float32).astype(jnp.bfloat16)
        moved = lax.all_to_all(
            hidden.reshape(step, n_dev, feat // n_dev), "tensor", 1, 1, tiled=True
        ).reshape(step, feat)
        active = jnp.maximum(moved, jnp.zeros((), jnp.bfloat16))
        gs = lax.dot_general(
            active, cot, (((0,), (0,)), ((), ())), preferred_element_type=jnp.float32
        )
        backed = jnp.dot(cot, w2p, preferred_element_type=jnp.float32)
        masked = jnp.where(moved > 0, backed, 0.0).astype(jnp.bfloat16)
        returned = lax.all_to_all(
            masked.reshape(step, n_dev, feat // n_dev), "tensor", 1, 1, tiled=True
        ).reshape(step, feat)
        gt = jnp.dot(returned, w1tp, preferred_element_type=jnp.float32).astype(jnp.bfloat16)
        outs.append(gt)
        gf = lax.dot_general(
            x, returned, (((0,), (0,)), ((), ())), preferred_element_type=jnp.float32
        )
        gf_acc = gf if gf_acc is None else gf_acc + gf
        gs_acc = gs if gs_acc is None else gs_acc + gs
    grad_tokens = jnp.concatenate(outs, axis=0)
    gf5 = gf_acc.reshape(blk_local, bs, NB, blk_local, sub)
    first_term = jnp.diagonal(gf5, axis1=0, axis2=3).transpose(3, 0, 1, 2)
    first_term = first_term.reshape(blk_local, bs, bs) * grad_scale
    gs6 = gs_acc.reshape(n_dev, blk_local, blk_local, sub, blk_local, bs)
    gsd = jnp.diagonal(gs6, axis1=1, axis2=4)
    second_term = gsd.transpose(4, 2, 0, 1, 3).reshape(blk_local, bs, bs) * grad_scale
    grad_first, grad_second = (
        lax.psum_scatter(first_term, "dp", scatter_dimension=1, tiled=True),
        lax.psum_scatter(second_term, "dp", scatter_dimension=1, tiled=True),
    )
    return (grad_tokens, grad_first, grad_second)


def solution(mesh):
    return jax.shard_map(
        shards,
        mesh=mesh,
        in_specs=(
            P(("groups", "dp"), "tensor"),
            P(("groups", "dp"), "tensor"),
            P("tensor", None, None),
            P("tensor", None, None),
        ),
        out_specs=(
            P(("groups", "dp"), "tensor"),
            P(("groups", "tensor"), "dp", None),
            P(("groups", "tensor"), "dp", None),
        ),
        check_vma=False,
    )
```

profile of v0, /device:TPU:0, one launch (start us, length us, event | category | flops | bytes accessed | tf_op | source)
XLA Modules:
  0.0 582.0 jit_solution(16535600350372632069)
XLA Ops:
  12.5 9.1 %convolution_convert_fusion.3 = bf16[1024,2048]{1,0:T(8,128)(2,1)} fusion(bf16[1024,1024]{0,1:T(8,128)(2,1)S(1)} %bitcast.136, bf16[8192,1024]{1,0:T(8,128)(2,1)} %param.4), kind=kOutput, calls=%fused_computation.18 | convolution fusion | flops 4297064448 | bytes 10485760 | tf_op jit(solution)/shard_map/dot_general | solution.py:47
  21.6 4.8 all-to-all-start.4
  26.5 9.3 %convolution_convert_fusion.5 = bf16[1024,2048]{1,0:T(8,128)(2,1)} fusion(bf16[1024,1024]{0,1:T(8,128)(2,1)} %bitcast.137, bf16[8192,1024]{1,0:T(8,128)(2,1)} %param.4), kind=kOutput, calls=%fused_computation.20 | convolution fusion | flops 4297064448 | bytes 10485760 | tf_op jit(solution)/shard_map/dot_general | solution.py:47
  35.8 39.5 %all-to-all-done.4 = bf16[2048,4,256]{0,2,1:T(8,128)(2,1)} async-done(((bf16[2048,4,256]{0,2,1:T(8,128)(2,1)}), bf16[2048,4,256]{0,2,1:T(8,128)(2,1)}, u32[]{:S(2)}, u32[]{:S(2)}) %all-to-all-start.4) | async-done | bytes 4194336 | tf_op jit(solution)/shard_map/all_to_all | solution.py:48
  75.3 5.3 all-to-all-start.2
  80.7 9.4 %convolution_convert_fusion.7 = bf16[1024,2048]{1,0:T(8,128)(2,1)} fusion(bf16[1024,1024]{0,1:T(8,128)(2,1)} %bitcast.138, bf16[8192,1024]{1,0:T(8,128)(2,1)} %param.4), kind=kOutput, calls=%fused_computation.22 | convolution fusion | flops 4297064448 | bytes 10485760 | tf_op jit(solution)/shard_map/dot_general | solution.py:47
  90.0 38.8 %all-to-all-done.2 = bf16[2048,4,256]{0,2,1:T(8,128)(2,1)} async-done(((bf16[2048,4,256]{0,2,1:T(8,128)(2,1)}), bf16[2048,4,256]{0,2,1:T(8,128)(2,1)}, u32[]{:S(2)}, u32[]{:S(2)}) %all-to-all-start.2) | async-done | bytes 4194336 | tf_op jit(solution)/shard_map/all_to_all | solution.py:48
  128.9 4.9 all-to-all-start
  140.0 8.3 %convolution_convert_fusion.1 = bf16[1024,2048]{1,0:T(8,128)(2,1)} fusion(bf16[1024,1024]{0,1:T(8,128)(2,1)S(1)} %bitcast.139, bf16[8192,1024]{1,0:T(8,128)(2,1)} %param.4), kind=kOutput, calls=%fused_computation.16 | convolution fusion | flops 4297064448 | bytes 10485760 | tf_op jit(solution)/shard_map/dot_general | solution.py:47
  148.3 33.7 %all-to-all-done = bf16[2048,4,256]{0,2,1:T(8,128)(2,1)} async-done(((bf16[2048,4,256]{0,2,1:T(8,128)(2,1)}), bf16[2048,4,256]{0,2,1:T(8,128)(2,1)}, u32[]{:S(2)}, u32[]{:S(2)}) %all-to-all-start) | async-done | bytes 4194336 | tf_op jit(solution)/shard_map/all_to_all | solution.py:48
  182.0 5.1 all-to-all-start.6
  187.0 4.4 broadcast_maximum_fusion.1
  191.5 4.5 broadcast_maximum_fusion.2
  199.2 3.4 broadcast_compare_fusion.2
  202.7 8.3 %fusion.1 = bf16[2048,1024]{0,1:T(8,128)(2,1)} fusion(pred[2048,4,256]{0,2,1:T(32,128)(4,1)S(1)} %broadcast_compare_fusion.1, bf16[1024,1024]{0,1:T(8,128)(2,1)S(1)} %bitcast.132, bf16[8192,1024]{1,0:T(8,128)(2,1)} %param.5), kind=kOutput, calls=%fused_computation.6 | convolution fusion | flops 4299161600 | bytes 12582912 | tf_op jit(solution)/shard_map/dot_general | solution.py:55
  210.9 24.3 %all-to-all-done.6 = bf16[2048,4,256]{0,2,1:T(8,128)(2,1)} async-done(((bf16[2048,4,256]{0,2,1:T(8,128)(2,1)}), bf16[2048,4,256]{0,2,1:T(8,128)(2,1)}, u32[]{:S(2)}, u32[]{:S(2)}) %all-to-all-start.6) | async-done | bytes 4194336 | tf_op jit(solution)/shard_map/all_to_all | solution.py:48
  235.3 4.8 all-to-all-start.5
  240.1 4.5 broadcast_maximum_fusion
  244.6 4.7 broadcast_compare_fusion
  249.3 8.5 %fusion.2 = bf16[2048,1024]{0,1:T(8,128)(2,1)} fusion(pred[2048,4,256]{0,2,1:T(32,128)(4,1)S(1)} %broadcast_compare_fusion.2, bf16[1024,1024]{0,1:T(8,128)(2,1)S(1)} %bitcast.133, bf16[8192,1024]{1,0:T(8,128)(2,1)} %param.5), kind=kOutput, calls=%fused_computation.8 | convolution fusion | flops 4299161600 | bytes 12582912 | tf_op jit(solution)/shard_map/dot_general | solution.py:55
  257.8 8.2 %fusion.10 = f32[1024,1024]{1,0:T(8,128)} fusion(bf16[2048,1024]{0,1:T(8,128)(2,1)S(1)} %bitcast.117, bf16[8192,1024]{1,0:T(8,128)(2,1)} %param.5), kind=kOutput, calls=%fused_computation.29 | convolution fusion | flops 4294967296 | bytes 12582912 | tf_op jit(solution)/shard_map/dot_general | solution.py:52
  266.0 22.3 %all-to-all-done.5 = bf16[2048,4,256]{0,2,1:T(8,128)(2,1)} async-done(((bf16[2048,4,256]{0,2,1:T(8,128)(2,1)}), bf16[2048,4,256]{0,2,1:T(8,128)(2,1)}, u32[]{:S(2)}, u32[]{:S(2)}) %all-to-all-start.5) | async-done | bytes 4194336 | tf_op jit(solution)/shard_map/all_to_all | solution.py:57
  288.3 5.3 all-to-all-start.3
  293.6 4.6 broadcast_maximum_fusion.3
  298.2 8.4 %fusion = bf16[2048,1024]{0,1:T(8,128)(2,1)} fusion(pred[2048,4,256]{0,2,1:T(32,128)(4,1)S(1)} %copy-done.6, bf16[1024,1024]{0,1:T(8,128)(2,1)S(1)} %bitcast.134, bf16[8192,1024]{1,0:T(8,128)(2,1)} %param.5), kind=kOutput, calls=%fused_computation.4 | convolution fusion | flops 4299161600 | bytes 12582912 | tf_op jit(solution)/shard_map/dot_general | solution.py:55
  306.6 8.3 %fusion.16 = f32[1024,1024]{1,0:T(8,128)} fusion(bf16[2048,1024]{0,1:T(8,128)(2,1)S(1)} %bitcast.115, bf16[8192,1024]{1,0:T(8,128)(2,1)} %param.5), kind=kOutput, calls=%fused_computation.35 | convolution fusion | flops 4294967296 | bytes 12582912 | tf_op jit(solution)/shard_map/dot_general | solution.py:52
  315.0 8.2 %fusion.4 = f32[1024,1024]{1,0:T(8,128)} fusion(bf16[2048,1024]{0,1:T(8,128)(2,1)S(1)} %bitcast.118, bf16[8192,1024]{1,0:T(8,128)(2,1)} %param.5), kind=kOutput, calls=%fused_computation.23 | convolution fusion | flops 4294967296 | bytes 12582912 | tf_op jit(solution)/shard_map/dot_general | solution.py:52
  323.2 18.6 %all-to-all-done.3 = bf16[2048,4,256]{0,2,1:T(8,128)(2,1)} async-done(((bf16[2048,4,256]{0,2,1:T(8,128)(2,1)}), bf16[2048,4,256]{0,2,1:T(8,128)(2,1)}, u32[]{:S(2)}, u32[]{:S(2)}) %all-to-all-start.3) | async-done | bytes 4194336 | tf_op jit(solution)/shard_map/all_to_all | solution.py:57
  341.8 4.9 all-to-all-start.7
  346.7 13.7 %add_add_fusion = f32[1024,1024]{1,0:T(8,128)} fusion(f32[1024,1024]{1,0:T(8,128)} %fusion.4, f32[1024,1024]{1,0:T(8,128)} %fusion.10, f32[1024,1024]{1,0:T(8,128)} %fusion.16, bf16[2048,1024]{0,1:T(8,128)(2,1)} %bitcast.123, bf16[8192,1024]{1,0:T(8,128)(2,1)} %param.5), kind=kOutput, calls=%fused_computation.13 | convolution fusion | flops 4298113024 | bytes 25165824 | tf_op jit(solution)/shard_map/dot_general | solution.py:52
  360.3 5.6 reshape.154
  366.0 5.1 copy.48
  375.7 3.3 broadcast_compare_fusion.3
  379.0 8.4 %fusion.3 = bf16[2048,1024]{0,1:T(8,128)(2,1)} fusion(pred[2048,4,256]{0,2,1:T(32,128)(4,1)S(1)} %broadcast_compare_fusion.3, bf16[1024,1024]{0,1:T(8,128)(2,1)S(1)} %bitcast.135, bf16[8192,1024]{1,0:T(8,128)(2,1)} %param.5), kind=kOutput, calls=%fused_computation.10 | convolution fusion | flops 4299161600 | bytes 12582912 | tf_op jit(solution)/shard_map/dot_general | solution.py:55
  387.3 10.0 %fusion.13 = f32[1024,1024]{1,0:T(8,128)} fusion(bf16[2048,1024]{0,1:T(8,128)(2,1)} %bitcast.21, bf16[8192,1024]{1,0:T(8,128)(2,1)} %param.4), kind=kOutput, calls=%fused_computation.32 | convolution fusion | flops 4294967296 | bytes 12582912 | tf_op jit(solution)/shard_map/dot_general | solution.py:62
  397.3 5.0 all-to-all-start.1
  402.6 8.5 %convolution_convert_fusion.2 = bf16[2048,1024]{1,0:T(8,128)(2,1)} fusion(bf16[2048,1024]{0,1:T(8,128)(2,1)} %bitcast.21, bf16[1024,1024]{1,0:T(8,128)(2,1)S(1)} %bitcast.129), kind=kOutput, calls=%fused_computation.17 | convolution fusion | flops 4297064448 | bytes 10485760 | tf_op jit(solution)/shard_map/dot_general | solution.py:60
  411.0 8.5 %convolution_convert_fusion.4 = bf16[2048,1024]{1,0:T(8,128)(2,1)} fusion(bf16[2048,1024]{0,1:T(8,128)(2,1)} %bitcast.15, bf16[1024,1024]{1,0:T(8,128)(2,1)S(1)} %bitcast.130), kind=kOutput, calls=%fused_computation.19 | convolution fusion | flops 4297064448 | bytes 10485760 | tf_op jit(solution)/shard_map/dot_general | solution.py:60
  419.6 8.3 %fusion.19 = f32[1024,1024]{1,0:T(8,128)} fusion(bf16[2048,1024]{0,1:T(8,128)(2,1)} %bitcast.15, bf16[8192,1024]{1,0:T(8,128)(2,1)S(1)} %bitcast.142), kind=kOutput, calls=%fused_computation.38 | convolution fusion | flops 4294967296 | bytes 12582912 | tf_op jit(solution)/shard_map/dot_general | solution.py:62
  427.9 8.2 %fusion.7 = f32[1024,1024]{1,0:T(8,128)} fusion(bf16[2048,1024]{0,1:T(8,128)(2,1)} %bitcast.27, bf16[8192,1024]{1,0:T(8,128)(2,1)S(1)} %bitcast.142), kind=kOutput, calls=%fused_computation.26 | convolution fusion | flops 4294967296 | bytes 12582912 | tf_op jit(solution)/shard_map/dot_general | solution.py:62
  436.1 14.4 %all-to-all-done.1 = bf16[2048,4,256]{0,2,1:T(8,128)(2,1)} async-done(((bf16[2048,4,256]{0,2,1:T(8,128)(2,1)}), bf16[2048,4,256]{0,2,1:T(8,128)(2,1)}, u32[]{:S(2)}, u32[]{:S(2)}) %all-to-all-start.1) | async-done | bytes 4194336 | tf_op jit(solution)/shard_map/all_to_all | solution.py:57
  450.5 8.7 %convolution_convert_fusion.6 = bf16[2048,1024]{1,0:T(8,128)(2,1)} fusion(bf16[2048,1024]{0,1:T(8,128)(2,1)} %bitcast.7, bf16[1024,1024]{1,0:T(8,128)(2,1)S(1)} %bitcast.131), kind=kOutput, calls=%fused_computation.21 | convolution fusion | flops 4297064448 | bytes 10485760 | tf_op jit(solution)/shard_map/dot_general | solution.py:60
  459.3 10.0 %add_bitcast_fusion = f32[1024,1024]{0,1:T(8,128)} fusion(f32[1024,1024]{1,0:T(8,128)S(1)} %copy-done.16, f32[1024,1024]{1,0:T(8,128)S(1)} %copy-done.14, f32[1024,1024]{1,0:T(8,128)S(1)} %copy-done.15, bf16[2048,1024]{0,1:T(8,128)(2,1)} %bitcast.7, bf16[8192,1024]{1,0:T(8,128)(2,1)} %param.4), kind=kOutput, calls=%fused_computation.14 | convolution fusion | flops 4298113024 | bytes 25165824 | tf_op jit(solution)/shard_map/dot_general | solution.py:62
  469.2 5.6 reshape.153
  474.9 4.9 copy.49
  484.0 7.6 %convolution_convert_fusion = bf16[2048,1024]{1,0:T(8,128)(2,1)S(1)} fusion(bf16[2048,1024]{0,1:T(8,128)(2,1)} %bitcast.27, bf16[1024,1024]{1,0:T(8,128)(2,1)} %bitcast.128), kind=kOutput, calls=%fused_computation.15 | convolution fusion | flops 4297064448 | bytes 10485760 | tf_op jit(solution)/shard_map/dot_general | solution.py:60
  491.6 8.5 %pad_maximum_fusion = bf16[8192,1024]{1,0:T(8,128)(2,1)} fusion(bf16[2048,1024]{1,0:T(8,128)(2,1)S(1)} %convolution_convert_fusion, bf16[2048,1024]{1,0:T(8,128)(2,1)S(1)} %copy-done.3, bf16[2048,1024]{1,0:T(8,128)(2,1)S(1)} %copy-done.4, bf16[2048,1024]{1,0:T(8,128)(2,1)S(1)} %copy-done.5), kind=kLoop, calls=%fused_computation.2 | loop fusion | flops 67108864 | bytes 33554432 | tf_op jit(solution)/shard_map/concatenate | solution.py:67
  500.2 72.2 %all-reduce.5.cloned.1.call-done = (f32[4,256,256]{2,0,1:T(4,128)}, f32[4,256,256]{2,0,1:T(4,128)}) async-done(((f32[4,256,256]{2,0,1:T(4,128)}, f32[4,256,256]{2,0,1:T(4,128)}), (f32[4,256,256]{2,0,1:T(4,128)}, f32[4,256,256]{2,0,1:T(4,128)})) %all-reduce.5.cloned.1.call-update) | async-done | bytes 2097168
  (70 shorter events, 25.8 us)
Async XLA Ops:
  12.5 9.1 %copy-start.11 = (bf16[128,8,4,256]{3,1,2,0:T(8,128)(2,1)}, bf16[128,8,4,256]{3,1,2,0:T(8,128)(2,1)S(1)}, u32[]{:S(2)}) copy-start(bf16[128,8,4,256]{3,1,2,0:T(8,128)(2,1)S(1)} %copy.43) | copy-start | bytes 6291460
  21.6 53.7 %all-to-all-start.4 = ((bf16[2048,4,256]{0,2,1:T(8,128)(2,1)}), bf16[2048,4,256]{0,2,1:T(8,128)(2,1)}, u32[]{:S(2)}, u32[]{:S(2)}) async-start(bf16[2048,4,256]{0,2,1:T(8,128)(2,1)} %bitcast.125), calls=%async_computation.4 | async-start | bytes 8388608 | tf_op jit(solution)/shard_map/all_to_all | solution.py:48
  75.3 53.5 %all-to-all-start.2 = ((bf16[2048,4,256]{0,2,1:T(8,128)(2,1)}), bf16[2048,4,256]{0,2,1:T(8,128)(2,1)}, u32[]{:S(2)}, u32[]{:S(2)}) async-start(bf16[2048,4,256]{0,2,1:T(8,128)(2,1)} %bitcast.124), calls=%async_computation.2 | async-start | bytes 8388608 | tf_op jit(solution)/shard_map/all_to_all | solution.py:48
  128.9 53.1 %all-to-all-start = ((bf16[2048,4,256]{0,2,1:T(8,128)(2,1)}), bf16[2048,4,256]{0,2,1:T(8,128)(2,1)}, u32[]{:S(2)}, u32[]{:S(2)}) async-start(bf16[2048,4,256]{0,2,1:T(8,128)(2,1)} %bitcast.114), calls=%async_computation | async-start | bytes 8388608 | tf_op jit(solution)/shard_map/all_to_all | solution.py:48
  135.7 3.0 copy-start.13
  135.7 4.3 copy-start.12
  182.0 53.3 %all-to-all-start.6 = ((bf16[2048,4,256]{0,2,1:T(8,128)(2,1)}), bf16[2048,4,256]{0,2,1:T(8,128)(2,1)}, u32[]{:S(2)}, u32[]{:S(2)}) async-start(bf16[2048,4,256]{0,2,1:T(8,128)(2,1)} %bitcast.121), calls=%async_computation.6 | async-start | bytes 8388608 | tf_op jit(solution)/shard_map/all_to_all | solution.py:48
  199.2 3.4 copy-start.8
  235.3 53.1 %all-to-all-start.5 = ((bf16[2048,4,256]{0,2,1:T(8,128)(2,1)}), bf16[2048,4,256]{0,2,1:T(8,128)(2,1)}, u32[]{:S(2)}, u32[]{:S(2)}) async-start(bf16[2048,4,256]{0,2,1:T(8,128)(2,1)} %bitcast.122), calls=%async_computation.5 | async-start | bytes 8388608 | tf_op jit(solution)/shard_map/all_to_all | solution.py:57
  244.6 4.7 copy-start.9
  249.3 8.5 %copy-start.1 = (bf16[2048,4,256]{0,2,1:T(8,128)(2,1)S(1)}, bf16[2048,4,256]{0,2,1:T(8,128)(2,1)}, u32[]{:S(2)}) copy-start(bf16[2048,4,256]{0,2,1:T(8,128)(2,1)} %broadcast_maximum_fusion.1) | copy-start | bytes 12582916
  288.3 53.5 %all-to-all-start.3 = ((bf16[2048,4,256]{0,2,1:T(8,128)(2,1)}), bf16[2048,4,256]{0,2,1:T(8,128)(2,1)}, u32[]{:S(2)}, u32[]{:S(2)}) async-start(bf16[2048,4,256]{0,2,1:T(8,128)(2,1)} %bitcast.120), calls=%async_computation.3 | async-start | bytes 8388608 | tf_op jit(solution)/shard_map/all_to_all | solution.py:57
  293.6 4.6 copy-start.6
  293.6 4.6 copy-start.10
  298.2 8.4 %copy-start = (bf16[2048,4,256]{0,2,1:T(8,128)(2,1)S(1)}, bf16[2048,4,256]{0,2,1:T(8,128)(2,1)}, u32[]{:S(2)}) copy-start(bf16[2048,4,256]{0,2,1:T(8,128)(2,1)} %broadcast_maximum_fusion.2) | copy-start | bytes 12582916
  306.6 8.4 %copy-start.2 = (bf16[2048,4,256]{0,2,1:T(8,128)(2,1)S(1)}, bf16[2048,4,256]{0,2,1:T(8,128)(2,1)}, u32[]{:S(2)}) copy-start(bf16[2048,4,256]{0,2,1:T(8,128)(2,1)} %broadcast_maximum_fusion) | copy-start | bytes 12582916
  341.8 55.5 %all-to-all-start.7 = ((bf16[2048,4,256]{0,2,1:T(8,128)(2,1)}), bf16[2048,4,256]{0,2,1:T(8,128)(2,1)}, u32[]{:S(2)}, u32[]{:S(2)}) async-start(bf16[2048,4,256]{0,2,1:T(8,128)(2,1)} %bitcast.116), calls=%async_computation.7 | async-start | bytes 8388608 | tf_op jit(solution)/shard_map/all_to_all | solution.py:57
  397.3 5.2 copy-start.7
  397.3 53.2 %all-to-all-start.1 = ((bf16[2048,4,256]{0,2,1:T(8,128)(2,1)}), bf16[2048,4,256]{0,2,1:T(8,128)(2,1)}, u32[]{:S(2)}, u32[]{:S(2)}) async-start(bf16[2048,4,256]{0,2,1:T(8,128)(2,1)} %bitcast.119), calls=%async_computation.1 | async-start | bytes 8388608 | tf_op jit(solution)/shard_map/all_to_all | solution.py:57
  402.3 170.0 %all-reduce.5.cloned.1.call-start = ((), (), s32[]{:S(2)}) async-start(), calls=%async_computation.8 | async-start | bytes 4194304
  402.5 17.0 %slice-start = ((s8[16777216]{0:T(1024)(128)(4,1)}), s8[4194304]{0:T(1024)(128)(4,1)S(1)}, s32[]{:S(2)}) async-start(s8[16777216]{0:T(1024)(128)(4,1)} %bitcast.141), calls=%async_computation.9 | async-start | bytes 8388608
  402.6 17.0 %slice-start.1 = ((s8[16777216]{0:T(1024)(128)(4,1)}), s8[4194304]{0:T(1024)(128)(4,1)S(1)}, s32[]{:S(2)}) async-start(s8[16777216]{0:T(1024)(128)(4,1)} %bitcast.141), calls=%async_computation.10 | async-start | bytes 8388608
  411.0 8.6 %slice-start.2 = ((s8[16777216]{0:T(1024)(128)(4,1)}), s8[4194304]{0:T(1024)(128)(4,1)S(1)}, s32[]{:S(2)}) async-start(s8[16777216]{0:T(1024)(128)(4,1)} %bitcast.141), calls=%async_computation.11 | async-start | bytes 8388608
  411.0 8.6 %slice-start.3 = ((s8[16777216]{0:T(1024)(128)(4,1)}), s8[4194304]{0:T(1024)(128)(4,1)S(1)}, s32[]{:S(2)}) async-start(s8[16777216]{0:T(1024)(128)(4,1)} %bitcast.141), calls=%async_computation.12 | async-start | bytes 8388608
  450.5 8.7 %copy-start.14 = (f32[1024,1024]{1,0:T(8,128)S(1)}, f32[1024,1024]{1,0:T(8,128)}, u32[]{:S(2)}) copy-start(f32[1024,1024]{1,0:T(8,128)} %fusion.13) | copy-start | bytes 12582916
  450.5 8.7 %copy-start.15 = (f32[1024,1024]{1,0:T(8,128)S(1)}, f32[1024,1024]{1,0:T(8,128)}, u32[]{:S(2)}) copy-start(f32[1024,1024]{1,0:T(8,128)} %fusion.19) | copy-start | bytes 12582916
  450.5 8.7 %copy-start.16 = (f32[1024,1024]{1,0:T(8,128)S(1)}, f32[1024,1024]{1,0:T(8,128)}, u32[]{:S(2)}) copy-start(f32[1024,1024]{1,0:T(8,128)} %fusion.7) | copy-start | bytes 12582916
  484.0 7.6 %copy-start.3 = (bf16[2048,1024]{1,0:T(8,128)(2,1)S(1)}, bf16[2048,1024]{1,0:T(8,128)(2,1)}, u32[]{:S(2)}) copy-start(bf16[2048,1024]{1,0:T(8,128)(2,1)} %convolution_convert_fusion.2) | copy-start | bytes 12582916
  484.0 7.6 %copy-start.4 = (bf16[2048,1024]{1,0:T(8,128)(2,1)S(1)}, bf16[2048,1024]{1,0:T(8,128)(2,1)}, u32[]{:S(2)}) copy-start(bf16[2048,1024]{1,0:T(8,128)(2,1)} %convolution_convert_fusion.4) | copy-start | bytes 12582916
  484.0 7.6 %copy-start.5 = (bf16[2048,1024]{1,0:T(8,128)(2,1)S(1)}, bf16[2048,1024]{1,0:T(8,128)(2,1)}, u32[]{:S(2)}) copy-start(bf16[2048,1024]{1,0:T(8,128)(2,1)} %convolution_convert_fusion.6) | copy-start | bytes 12582916
Sparse Core Ops, SparseCore 0:
  484.1 88.1 all-reduce.4
where the time goes:
time: 590 us; the launch traced here: 582 us
  waiting for transfers between devices  264 us (45%)
  matrix products  178 us (30%)
  other arithmetic  43.8 us (7%)
  local copies, waits for them, and re-layouts  40.9 us (7%)
  starting transfers between devices  40.3 us (7%)
  between operations  15.3 us (3%)
    all_to_all x4, waiting for transfers between devices, shards(): lax.all_to_all(hidden.reshape(step, n_dev, feat // n_dev), 'tensor', 1, 1...  136 us
    unnamed x2, waiting for transfers between devices  72.2 us
    all_to_all x4, waiting for transfers between devices, shards(): lax.all_to_all(masked.reshape(step, n_dev, feat // n_dev), 'tensor', 1, 1...  55.3 us
    dot_general x4, matrix products, shards(): lax.dot_general(active, cot, (((0,), (0,)), ((), ())), preferred_element_...  38.4 us
    dot_general x4, matrix products, shards(): lax.dot_general(x, returned, (((0,), (0,)), ((), ())), preferred_element_...  36.4 us
    dot_general x4, matrix products, shards(): jnp.dot(x, w1p, preferred_element_type=jnp.float32).astype(jnp.bfloat16)  36.1 us
    dot_general x4, matrix products, shards(): backed = jnp.dot(cot, w2p, preferred_element_type=jnp.float32)  33.5 us
    dot_general x4, matrix products, shards(): jnp.dot(returned, w1tp, preferred_element_type=jnp.float32)  33.3 us
  transfers between devices with their start and end apart: 9, of which 8 were waited for; matrix products, arithmetic and copies ran while one was open for 36% of the time, Pallas kernels for 0%

commit v1 on v0

--- a/solution.py
+++ b/solution.py
@@ -6,6 +6,22 @@
 
 NB = 16
 CHUNKS = 4
+
+
+def pairwise_exchange(array, axis, split, join):
+    ways, here = (lax.axis_size(axis), lax.axis_index(axis))
+    width = array.shape[split] // ways
+    shape = list(array.shape)
+    shape[split] = width
+    height = shape[join]
+    shape[join] = height * ways
+    full = jnp.zeros(shape, array.dtype)
+    for mask in range(ways):
+        part = lax.dynamic_slice_in_dim(array, (here ^ mask) * width, width, axis=split)
+        if mask:
+            part = lax.ppermute(part, axis, [(d, d ^ mask) for d in range(ways)])
+        full = lax.dynamic_update_slice_in_dim(full, part, (here ^ mask) * height, axis=join)
+    return full
 
 
 def expanded_weights(w_first, w_second, n_dev):
@@ -45,8 +61,8 @@
         x = tokens[k * step : (k + 1) * step]
         cot = cotangent[k * step : (k + 1) * step]
         hidden = jnp.dot(x, w1p, preferred_element_type=jnp.float32).astype(jnp.bfloat16)
-        moved = lax.all_to_all(
-            hidden.reshape(step, n_dev, feat // n_dev), "tensor", 1, 1, tiled=True
+        moved = pairwise_exchange(
+            hidden.reshape(step, n_dev, feat // n_dev), "tensor", 1, 1
         ).reshape(step, feat)
         active = jnp.maximum(moved, jnp.zeros((), jnp.bfloat16))
         gs = lax.dot_general(

time: 590 us -> 569 us (0.964)
  local copies, waits for them, and re-layouts: 40.9 us -> 77.3 us
  waiting for transfers between devices: 264 us -> 243 us
  matrix products: 178 us -> 161 us
  starting transfers between devices: 40.3 us -> 28.3 us
  other arithmetic: 43.8 us -> 36.2 us
    all_to_all x4 -> x0, waiting for transfers between devices: 136 us -> none  [shards(): lax.all_to_all(hidden.reshape(step, n_dev, feat // n_dev), 'tensor', 1, 1...]
    ppermute x0 -> x12, waiting for transfers between devices: none -> 111 us  [pairwise_exchange(): part = lax.ppermute(part, axis, [(d, d ^ mask) for d in range(ways)])]
    all_to_all x4 -> x0, starting transfers between devices: 20.1 us -> none  [shards(): lax.all_to_all(hidden.reshape(step, n_dev, feat // n_dev), 'tensor', 1, 1...]
    dynamic_update_slice x0 -> x12, local copies, waits for them, and re-layouts: none -> 16.4 us  [pairwise_exchange(): lax.dynamic_update_slice_in_dim(full, part, (here ^ mask) * height, axis=...]
    dot_general x4, matrix products: 36.1 us -> 23.4 us  [shards(): jnp.dot(x, w1p, preferred_element_type=jnp.float32).astype(jnp.bfloat16)]
    ppermute x0 -> x12, starting transfers between devices: none -> 8.52 us  [pairwise_exchange(): part = lax.ppermute(part, axis, [(d, d ^ mask) for d in range(ways)])]
    another operation x0 -> x4, local copies, waits for them, and re-layouts: none -> 8.18 us
    dynamic_slice x0 -> x4, local copies, waits for them, and re-layouts: none -> 7.06 us  [pairwise_exchange(): lax.dynamic_slice_in_dim(array, (here ^ mask) * width, width, axis=split)]
  transfers between devices with their start and end apart: 9 -> 17, of which waited for: 8 -> 9; matrix products, arithmetic and copies ran while one was open for 36% -> 39% of each run, Pallas kernels for 0% -> 0%
where the time goes in v1:
time: 569 us; the launch traced here: 562 us
  waiting for transfers between devices  243 us (43%)
  matrix products  161 us (28%)
  local copies, waits for them, and re-layouts  77.3 us (14%)
  other arithmetic  36.2 us (6%)
  starting transfers between devices  28.3 us (5%)
  between operations  15.7 us (3%)
    ppermute x12, waiting for transfers between devices, pairwise_exchange(): part = lax.ppermute(part, axis, [(d, d ^ mask) for d in range(ways)])  111 us
    unnamed x2, waiting for transfers between devices  71.4 us
    all_to_all x4, waiting for transfers between devices, shards(): lax.all_to_all(masked.reshape(step, n_dev, feat // n_dev), 'tensor', 1, 1...  60.6 us
    dot_general x4, matrix products, shards(): lax.dot_general(x, returned, (((0,), (0,)), ((), ())), preferred_element_...  36.6 us
    dot_general x4, matrix products, shards(): backed = jnp.dot(cot, w2p, preferred_element_type=jnp.float32)  34 us
    dot_general x4, matrix products, shards(): lax.dot_general(active, cot, (((0,), (0,)), ((), ())), preferred_element_...  33.8 us
    dot_general x4, matrix products, shards(): jnp.dot(returned, w1tp, preferred_element_type=jnp.float32)  33.6 us
    dot_general x4, matrix products, shards(): jnp.dot(x, w1p, preferred_element_type=jnp.float32).astype(jnp.bfloat16)  23.4 us
  transfers between devices with their start and end apart: 17, of which 9 were waited for; matrix products, arithmetic and copies ran while one was open for 39% of the time, Pallas kernels for 0%

profile of v1, /device:TPU:0, one launch (start us, length us, event | category | flops | bytes accessed | tf_op | source)
XLA Modules:
  0.0 561.9 jit_solution(7357868802011594235)
XLA Ops:
  13.8 7.5 %convolution_convert_fusion.5 = bf16[1024,2048]{1,0:T(8,128)(2,1)S(1)} fusion(bf16[1024,1024]{0,1:T(8,128)(2,1)} %bitcast.136, bf16[8192,1024]{1,0:T(8,128)(2,1)} %param.4), kind=kOutput, calls=%fused_computation.20 | convolution fusion | flops 4297064448 | bytes 10485760 | tf_op jit(solution)/shard_map/dot_general | solution.py:63
  21.3 2.7 broadcast.73.clone.2
  29.3 5.0 convolution_convert_fusion.7
  40.9 4.8 convolution_convert_fusion.3
  45.7 6.1 %convolution_convert_fusion.1 = bf16[1024,2048]{1,0:T(8,128)(2,1)} fusion(bf16[1024,1024]{0,1:T(8,128)(2,1)S(1)} %bitcast.139, bf16[8192,1024]{1,0:T(8,128)(2,1)S(1)} %bitcast.144), kind=kOutput, calls=%fused_computation.16 | convolution fusion | flops 4297064448 | bytes 10485760 | tf_op jit(solution)/shard_map/dot_general | solution.py:63
  70.9 4.7 collective-permute-done.5
  79.5 3.3 broadcast_compare_fusion.2
  82.8 8.8 %fusion.2 = bf16[2048,1024]{0,1:T(8,128)(2,1)} fusion(pred[2048,4,256]{0,2,1:T(32,128)(4,1)S(1)} %broadcast_compare_fusion.2, bf16[1024,1024]{0,1:T(8,128)(2,1)S(1)} %bitcast.132, bf16[8192,1024]{1,0:T(8,128)(2,1)} %param.5), kind=kOutput, calls=%fused_computation.8 | convolution fusion | flops 4299161600 | bytes 12582912 | tf_op jit(solution)/shard_map/dot_general | solution.py:71
  92.9 50.3 %collective-permute-done.7 = bf16[2048,1,256]{0,2,1:T(8,128)(2,1)S(1)} collective-permute-done((bf16[2048,1,256]{0,2,1:T(8,128)(2,1)S(1)}, bf16[2048,1,256]{0,2,1:T(8,128)(2,1)S(1)}, u32[]{:S(2)}, u32[]{:S(2)}) %collective-permute-start.7) | collective-permute-done | bytes 1048608 | tf_op jit(solution)/shard_map/ppermute | solution.py:22
  144.4 4.5 broadcast_maximum_fusion.2
  148.9 16.5 %collective-permute-done.8 = bf16[2048,1,256]{0,2,1:T(8,128)(2,1)S(1)} collective-permute-done((bf16[2048,1,256]{0,2,1:T(8,128)(2,1)S(1)}, bf16[2048,1,256]{0,2,1:T(8,128)(2,1)S(1)}, u32[]{:S(2)}, u32[]{:S(2)}) %collective-permute-start.8) | collective-permute-done | bytes 1048608 | tf_op jit(solution)/shard_map/ppermute | solution.py:22
  168.1 4.4 broadcast_maximum_fusion.1
  172.5 18.9 %collective-permute-done.10 = bf16[2048,1,256]{0,2,1:T(8,128)(2,1)S(1)} collective-permute-done((bf16[2048,1,256]{0,2,1:T(8,128)(2,1)S(1)}, bf16[2048,1,256]{0,2,1:T(8,128)(2,1)S(1)}, u32[]{:S(2)}, u32[]{:S(2)}) %collective-permute-start.10) | collective-permute-done | bytes 1048608 | tf_op jit(solution)/shard_map/ppermute | solution.py:22
  191.5 20.7 %collective-permute-done.11 = bf16[2048,1,256]{0,2,1:T(8,128)(2,1)S(1)} collective-permute-done((bf16[2048,1,256]{0,2,1:T(8,128)(2,1)S(1)}, bf16[2048,1,256]{0,2,1:T(8,128)(2,1)S(1)}, u32[]{:S(2)}, u32[]{:S(2)}) %collective-permute-start.11) | collective-permute-done | bytes 1048608 | tf_op jit(solution)/shard_map/ppermute | solution.py:22
  212.3 2.5 broadcast_maximum_fusion
  215.6 4.8 all-to-all-start.1
  222.7 3.4 broadcast_compare_fusion.1
  230.7 8.4 %fusion.1 = bf16[2048,1024]{0,1:T(8,128)(2,1)} fusion(pred[2048,4,256]{0,2,1:T(32,128)(4,1)S(1)} %broadcast_compare_fusion.1, bf16[1024,1024]{0,1:T(8,128)(2,1)S(1)} %bitcast.133, bf16[8192,1024]{1,0:T(8,128)(2,1)} %param.5), kind=kOutput, calls=%fused_computation.6 | convolution fusion | flops 4299161600 | bytes 12582912 | tf_op jit(solution)/shard_map/dot_general | solution.py:71
  239.1 8.2 %fusion.16 = f32[1024,1024]{1,0:T(8,128)} fusion(bf16[2048,1024]{0,1:T(8,128)(2,1)S(1)} %bitcast.119, bf16[8192,1024]{1,0:T(8,128)(2,1)} %param.5), kind=kOutput, calls=%fused_computation.35 | convolution fusion | flops 4294967296 | bytes 12582912 | tf_op jit(solution)/shard_map/dot_general | solution.py:68
  247.3 21.5 %all-to-all-done.1 = bf16[2048,4,256]{0,2,1:T(8,128)(2,1)} async-done(((bf16[2048,4,256]{0,2,1:T(8,128)(2,1)}), bf16[2048,4,256]{0,2,1:T(8,128)(2,1)}, u32[]{:S(2)}, u32[]{:S(2)}) %all-to-all-start.1) | async-done | bytes 4194336 | tf_op jit(solution)/shard_map/all_to_all | solution.py:73
  268.8 4.9 all-to-all-start.2
  273.7 2.6 broadcast_maximum_fusion.3
  276.6 8.5 %fusion = bf16[2048,1024]{0,1:T(8,128)(2,1)} fusion(pred[2048,4,256]{0,2,1:T(32,128)(4,1)S(1)} %broadcast_compare_fusion, bf16[1024,1024]{0,1:T(8,128)(2,1)S(1)} %bitcast.134, bf16[8192,1024]{1,0:T(8,128)(2,1)} %param.5), kind=kOutput, calls=%fused_computation.4 | convolution fusion | flops 4299161600 | bytes 12582912 | tf_op jit(solution)/shard_map/dot_general | solution.py:71
  285.1 6.1 %fusion.22 = f32[1024,1024]{1,0:T(8,128)} fusion(bf16[2048,1024]{0,1:T(8,128)(2,1)S(1)} %bitcast.125, bf16[8192,1024]{1,0:T(8,128)(2,1)S(1)} %bitcast.142), kind=kOutput, calls=%fused_computation.41 | convolution fusion | flops 4294967296 | bytes 12582912 | tf_op jit(solution)/shard_map/dot_general | solution.py:68
  291.2 6.0 %fusion.10 = f32[1024,1024]{1,0:T(8,128)} fusion(bf16[2048,1024]{0,1:T(8,128)(2,1)S(1)} %bitcast.120, bf16[8192,1024]{1,0:T(8,128)(2,1)S(1)} %bitcast.142), kind=kOutput, calls=%fused_computation.29 | convolution fusion | flops 4294967296 | bytes 12582912 | tf_op jit(solution)/shard_map/dot_general | solution.py:68
  297.2 24.7 %all-to-all-done.2 = bf16[2048,4,256]{0,2,1:T(8,128)(2,1)} async-done(((bf16[2048,4,256]{0,2,1:T(8,128)(2,1)}), bf16[2048,4,256]{0,2,1:T(8,128)(2,1)}, u32[]{:S(2)}, u32[]{:S(2)}) %all-to-all-start.2) | async-done | bytes 4194336 | tf_op jit(solution)/shard_map/all_to_all | solution.py:73
  321.9 5.0 all-to-all-start.3
  327.0 13.5 %add_add_fusion = f32[1024,1024]{1,0:T(8,128)} fusion(f32[1024,1024]{1,0:T(8,128)} %fusion.10, f32[1024,1024]{1,0:T(8,128)} %fusion.22, f32[1024,1024]{1,0:T(8,128)} %fusion.16, bf16[2048,1024]{0,1:T(8,128)(2,1)} %bitcast.121, bf16[8192,1024]{1,0:T(8,128)(2,1)} %param.5), kind=kOutput, calls=%fused_computation.13 | convolution fusion | flops 4298113024 | bytes 25165824 | tf_op jit(solution)/shard_map/dot_general | solution.py:68
  340.5 5.6 reshape.154
  346.1 5.2 copy.48
  351.3 2.8 gather_fusion.1
  355.9 3.3 broadcast_compare_fusion.3
  359.2 8.3 %fusion.3 = bf16[2048,1024]{0,1:T(8,128)(2,1)} fusion(pred[2048,4,256]{0,2,1:T(32,128)(4,1)S(1)} %broadcast_compare_fusion.3, bf16[1024,1024]{0,1:T(8,128)(2,1)S(1)} %bitcast.135, bf16[8192,1024]{1,0:T(8,128)(2,1)} %param.5), kind=kOutput, calls=%fused_computation.10 | convolution fusion | flops 4299161600 | bytes 12582912 | tf_op jit(solution)/shard_map/dot_general | solution.py:71
  367.5 10.0 %fusion.19 = f32[1024,1024]{1,0:T(8,128)} fusion(bf16[2048,1024]{0,1:T(8,128)(2,1)} %bitcast.17, bf16[8192,1024]{1,0:T(8,128)(2,1)} %param.4), kind=kOutput, calls=%fused_computation.38 | convolution fusion | flops 4294967296 | bytes 12582912 | tf_op jit(solution)/shard_map/dot_general | solution.py:78
  377.5 5.0 all-to-all-start
  382.6 8.8 %convolution_convert_fusion.4 = bf16[2048,1024]{1,0:T(8,128)(2,1)} fusion(bf16[2048,1024]{0,1:T(8,128)(2,1)} %bitcast.17, bf16[1024,1024]{1,0:T(8,128)(2,1)S(1)} %bitcast.129), kind=kOutput, calls=%fused_computation.19 | convolution fusion | flops 4297064448 | bytes 10485760 | tf_op jit(solution)/shard_map/dot_general | solution.py:76
  391.4 8.4 %convolution_convert_fusion.2 = bf16[2048,1024]{1,0:T(8,128)(2,1)} fusion(bf16[2048,1024]{0,1:T(8,128)(2,1)} %bitcast.24, bf16[1024,1024]{1,0:T(8,128)(2,1)S(1)} %bitcast.130), kind=kOutput, calls=%fused_computation.17 | convolution fusion | flops 4297064448 | bytes 10485760 | tf_op jit(solution)/shard_map/dot_general | solution.py:76
  399.9 8.3 %fusion.13 = f32[1024,1024]{1,0:T(8,128)} fusion(bf16[2048,1024]{0,1:T(8,128)(2,1)} %bitcast.24, bf16[8192,1024]{1,0:T(8,128)(2,1)S(1)} %bitcast.146), kind=kOutput, calls=%fused_computation.32 | convolution fusion | flops 4294967296 | bytes 12582912 | tf_op jit(solution)/shard_map/dot_general | solution.py:78
  408.2 8.3 %fusion.7 = f32[1024,1024]{1,0:T(8,128)} fusion(bf16[2048,1024]{0,1:T(8,128)(2,1)} %bitcast.31, bf16[8192,1024]{1,0:T(8,128)(2,1)S(1)} %bitcast.146), kind=kOutput, calls=%fused_computation.26 | convolution fusion | flops 4294967296 | bytes 12582912 | tf_op jit(solution)/shard_map/dot_general | solution.py:78
  416.4 14.3 %all-to-all-done = bf16[2048,4,256]{0,2,1:T(8,128)(2,1)} async-done(((bf16[2048,4,256]{0,2,1:T(8,128)(2,1)}), bf16[2048,4,256]{0,2,1:T(8,128)(2,1)}, u32[]{:S(2)}, u32[]{:S(2)}) %all-to-all-start) | async-done | bytes 4194336 | tf_op jit(solution)/shard_map/all_to_all | solution.py:73
  430.8 8.8 %convolution_convert_fusion.6 = bf16[2048,1024]{1,0:T(8,128)(2,1)} fusion(bf16[2048,1024]{0,1:T(8,128)(2,1)} %bitcast.8, bf16[1024,1024]{1,0:T(8,128)(2,1)S(1)} %bitcast.131), kind=kOutput, calls=%fused_computation.21 | convolution fusion | flops 4297064448 | bytes 10485760 | tf_op jit(solution)/shard_map/dot_general | solution.py:76
  439.6 10.1 %add_bitcast_fusion = f32[1024,1024]{0,1:T(8,128)} fusion(f32[1024,1024]{1,0:T(8,128)S(1)} %copy-done.21, f32[1024,1024]{1,0:T(8,128)S(1)} %copy-done.20, f32[1024,1024]{1,0:T(8,128)S(1)} %copy-done.19, bf16[2048,1024]{0,1:T(8,128)(2,1)} %bitcast.8, bf16[8192,1024]{1,0:T(8,128)(2,1)} %param.4), kind=kOutput, calls=%fused_computation.14 | convolution fusion | flops 4298113024 | bytes 25165824 | tf_op jit(solution)/shard_map/dot_general | solution.py:78
  449.7 5.6 reshape.153
  455.3 5.0 copy.49
  460.2 2.8 gather_fusion
  464.5 7.6 %convolution_convert_fusion = bf16[2048,1024]{1,0:T(8,128)(2,1)S(1)} fusion(bf16[2048,1024]{0,1:T(8,128)(2,1)} %bitcast.31, bf16[1024,1024]{1,0:T(8,128)(2,1)} %bitcast.128), kind=kOutput, calls=%fused_computation.15 | convolution fusion | flops 4297064448 | bytes 10485760 | tf_op jit(solution)/shard_map/dot_general | solution.py:76
  472.1 8.5 %pad_maximum_fusion = bf16[8192,1024]{1,0:T(8,128)(2,1)} fusion(bf16[2048,1024]{1,0:T(8,128)(2,1)S(1)} %convolution_convert_fusion, bf16[2048,1024]{1,0:T(8,128)(2,1)S(1)} %copy-done.6, bf16[2048,1024]{1,0:T(8,128)(2,1)S(1)} %copy-done.5, bf16[2048,1024]{1,0:T(8,128)(2,1)S(1)} %copy-done.7), kind=kLoop, calls=%fused_computation.2 | loop fusion | flops 67108864 | bytes 33554432 | tf_op jit(solution)/shard_map/concatenate | solution.py:83
  480.7 71.4 %all-reduce.5.cloned.1.call-done = (f32[4,256,256]{2,0,1:T(4,128)}, f32[4,256,256]{2,0,1:T(4,128)}) async-done(((f32[4,256,256]{2,0,1:T(4,128)}, f32[4,256,256]{2,0,1:T(4,128)}), (f32[4,256,256]{2,0,1:T(4,128)}, f32[4,256,256]{2,0,1:T(4,128)})) %all-reduce.5.cloned.1.call-update) | async-done | bytes 2097168
  (134 shorter events, 60.0 us)
Async XLA Ops:
  13.8 15.5 %slice-start.4 = ((s8[16777216]{0:T(1024)(128)(4,1)}), s8[4194304]{0:T(1024)(128)(4,1)S(1)}, s32[]{:S(2)}) async-start(s8[16777216]{0:T(1024)(128)(4,1)} %bitcast.143), calls=%async_computation.9 | async-start | bytes 8388608
  13.8 15.5 %slice-start.5 = ((s8[16777216]{0:T(1024)(128)(4,1)}), s8[4194304]{0:T(1024)(128)(4,1)S(1)}, s32[]{:S(2)}) async-start(s8[16777216]{0:T(1024)(128)(4,1)} %bitcast.143), calls=%async_computation.10 | async-start | bytes 8388608
  13.8 15.5 %slice-start.6 = ((s8[16777216]{0:T(1024)(128)(4,1)}), s8[4194304]{0:T(1024)(128)(4,1)S(1)}, s32[]{:S(2)}) async-start(s8[16777216]{0:T(1024)(128)(4,1)} %bitcast.143), calls=%async_computation.11 | async-start | bytes 8388608
  21.3 8.0 %slice-start.7 = ((s8[16777216]{0:T(1024)(128)(4,1)}), s8[4194304]{0:T(1024)(128)(4,1)S(1)}, s32[]{:S(2)}) async-start(s8[16777216]{0:T(1024)(128)(4,1)} %bitcast.143), calls=%async_computation.12 | async-start | bytes 8388608
  24.0 5.3 copy-start.13
  26.2 39.3 %collective-permute-start.3 = (bf16[2048,1,256]{0,2,1:T(8,128)(2,1)}, bf16[2048,1,256]{0,2,1:T(8,128)(2,1)}, u32[]{:S(2)}, u32[]{:S(2)}) collective-permute-start(bf16[2048,1,256]{0,2,1:T(8,128)(2,1)} %get-tuple-element.20), channel_id=1, source_target_pairs={{0,4},{4,0},{8,12},{12,8},{1,5},{5,1},{9,13},{13,9},{2,6},{6,2},{1... | collective-permute-start | bytes 3145736 | tf_op jit(solution)/shard_map/ppermute | solution.py:22
  26.7 41.8 %collective-permute-start.4 = (bf16[2048,1,256]{0,2,1:T(8,128)(2,1)}, bf16[2048,1,256]{0,2,1:T(8,128)(2,1)}, u32[]{:S(2)}, u32[]{:S(2)}) collective-permute-start(bf16[2048,1,256]{0,2,1:T(8,128)(2,1)} %get-tuple-element.19), channel_id=1, source_target_pairs={{0,8},{4,12},{8,0},{12,4},{1,9},{5,13},{9,1},{13,5},{2,10},{6,14},... | collective-permute-start | bytes 3145736 | tf_op jit(solution)/shard_map/ppermute | solution.py:22
  29.1 46.4 %collective-permute-start.5 = (bf16[2048,1,256]{0,2,1:T(8,128)(2,1)}, bf16[2048,1,256]{0,2,1:T(8,128)(2,1)}, u32[]{:S(2)}, u32[]{:S(2)}) collective-permute-start(bf16[2048,1,256]{0,2,1:T(8,128)(2,1)} %get-tuple-element.18), channel_id=1, source_target_pairs={{0,12},{4,8},{8,4},{12,0},{1,13},{5,9},{9,5},{13,1},{2,14},{6,10},... | collective-permute-start | bytes 3145736 | tf_op jit(solution)/shard_map/ppermute | solution.py:22
  38.9 181.5 %collective-permute-start = (bf16[2048,1,256]{0,2,1:T(8,128)(2,1)}, bf16[2048,1,256]{0,2,1:T(8,128)(2,1)}, u32[]{:S(2)}, u32[]{:S(2)}) collective-permute-start(bf16[2048,1,256]{0,2,1:T(8,128)(2,1)} %get-tuple-element.16), channel_id=1, source_target_pairs={{0,4},{4,0},{8,12},{12,8},{1,5},{5,1},{9,13},{13,9},{2,6},{6,2},{1... | collective-permute-start | bytes 3145736 | tf_op jit(solution)/shard_map/ppermute | solution.py:22
  39.0 187.1 %collective-permute-start.1 = (bf16[2048,1,256]{0,2,1:T(8,128)(2,1)}, bf16[2048,1,256]{0,2,1:T(8,128)(2,1)}, u32[]{:S(2)}, u32[]{:S(2)}) collective-permute-start(bf16[2048,1,256]{0,2,1:T(8,128)(2,1)} %get-tuple-element.15), channel_id=1, source_target_pairs={{0,8},{4,12},{8,0},{12,4},{1,9},{5,13},{9,1},{13,5},{2,10},{6,14},... | collective-permute-start | bytes 3145736 | tf_op jit(solution)/shard_map/ppermute | solution.py:22
  57.8 3.7 copy-start.18
  64.9 3.6 copy-start.17
  65.5 10.0 %copy-start.16 = (bf16[2048,1,256]{0,2,1:T(8,128)(2,1)S(1)}, bf16[2048,1,256]{0,2,1:T(8,128)(2,1)}, u32[]{:S(2)}) copy-start(bf16[2048,1,256]{0,2,1:T(8,128)(2,1)} %get-tuple-element.23) | copy-start | bytes 3145732
  66.2 162.3 %collective-permute-start.2 = (bf16[2048,1,256]{0,2,1:T(8,128)(2,1)S(1)}, bf16[2048,1,256]{0,2,1:T(8,128)(2,1)S(1)}, u32[]{:S(2)}, u32[]{:S(2)}) collective-permute-start(bf16[2048,1,256]{0,2,1:T(8,128)(2,1)S(1)} %copy-done.14), channel_id=1, source_target_pairs={{0,12},{4,8},{8,4},{12,0},{1,13},{5,9},{9,5},{13,1},{2,14},{6,10},... | collective-permute-start | bytes 3145736 | tf_op jit(solution)/shard_map/ppermute | solution.py:22
  68.5 23.1 %collective-permute-start.6 = (bf16[2048,1,256]{0,2,1:T(8,128)(2,1)S(1)}, bf16[2048,1,256]{0,2,1:T(8,128)(2,1)S(1)}, u32[]{:S(2)}, u32[]{:S(2)}) collective-permute-start(bf16[2048,1,256]{0,2,1:T(8,128)(2,1)S(1)} %copy-done.17), channel_id=1, source_target_pairs={{0,4},{4,0},{8,12},{12,8},{1,5},{5,1},{9,13},{13,9},{2,6},{6,2},{1... | collective-permute-start | bytes 3145736 | tf_op jit(solution)/shard_map/ppermute | solution.py:22
  75.6 7.2 %copy-start.9 = (bf16[128,8,4,256]{3,1,2,0:T(8,128)(2,1)S(1)}, bf16[128,8,4,256]{3,1,2,0:T(8,128)(2,1)}, u32[]{:S(2)}) copy-start(bf16[128,8,4,256]{3,1,2,0:T(8,128)(2,1)} %copy.44) | copy-start | bytes 6291460
  75.6 67.7 %collective-permute-start.7 = (bf16[2048,1,256]{0,2,1:T(8,128)(2,1)S(1)}, bf16[2048,1,256]{0,2,1:T(8,128)(2,1)S(1)}, u32[]{:S(2)}, u32[]{:S(2)}) collective-permute-start(bf16[2048,1,256]{0,2,1:T(8,128)(2,1)S(1)} %copy-done.16), channel_id=1, source_target_pairs={{0,8},{4,12},{8,0},{12,4},{1,9},{5,13},{9,1},{13,5},{2,10},{6,14},... | collective-permute-start | bytes 3145736 | tf_op jit(solution)/shard_map/ppermute | solution.py:22
  82.8 8.8 %copy-start.15 = (bf16[2048,1,256]{0,2,1:T(8,128)(2,1)S(1)}, bf16[2048,1,256]{0,2,1:T(8,128)(2,1)}, u32[]{:S(2)}) copy-start(bf16[2048,1,256]{0,2,1:T(8,128)(2,1)} %get-tuple-element.22) | copy-start | bytes 3145732
  91.6 73.8 %collective-permute-start.8 = (bf16[2048,1,256]{0,2,1:T(8,128)(2,1)S(1)}, bf16[2048,1,256]{0,2,1:T(8,128)(2,1)S(1)}, u32[]{:S(2)}, u32[]{:S(2)}) collective-permute-start(bf16[2048,1,256]{0,2,1:T(8,128)(2,1)S(1)} %copy-done.15), channel_id=1, source_target_pairs={{0,12},{4,8},{8,4},{12,0},{1,13},{5,9},{9,5},{13,1},{2,14},{6,10},... | collective-permute-start | bytes 3145736 | tf_op jit(solution)/shard_map/ppermute | solution.py:22
  143.2 24.7 %collective-permute-start.9 = (bf16[2048,1,256]{0,2,1:T(8,128)(2,1)S(1)}, bf16[2048,1,256]{0,2,1:T(8,128)(2,1)S(1)}, u32[]{:S(2)}, u32[]{:S(2)}) collective-permute-start(bf16[2048,1,256]{0,2,1:T(8,128)(2,1)S(1)} %get-tuple-element.28), channel_id=1, source_target_pairs={{0,4},{4,0},{8,12},{12,8},{1,5},{5,1},{9,13},{13,9},{2,6},{6,2},{1... | collective-permute-start | bytes 3145736 | tf_op jit(solution)/shard_map/ppermute | solution.py:22
  165.3 26.0 %collective-permute-start.10 = (bf16[2048,1,256]{0,2,1:T(8,128)(2,1)S(1)}, bf16[2048,1,256]{0,2,1:T(8,128)(2,1)S(1)}, u32[]{:S(2)}, u32[]{:S(2)}) collective-permute-start(bf16[2048,1,256]{0,2,1:T(8,128)(2,1)S(1)} %get-tuple-element.27), channel_id=1, source_target_pairs={{0,8},{4,12},{8,0},{12,4},{1,9},{5,13},{9,1},{13,5},{2,10},{6,14},... | collective-permute-start | bytes 3145736 | tf_op jit(solution)/shard_map/ppermute | solution.py:22
  168.0 44.2 %collective-permute-start.11 = (bf16[2048,1,256]{0,2,1:T(8,128)(2,1)S(1)}, bf16[2048,1,256]{0,2,1:T(8,128)(2,1)S(1)}, u32[]{:S(2)}, u32[]{:S(2)}) collective-permute-start(bf16[2048,1,256]{0,2,1:T(8,128)(2,1)S(1)} %get-tuple-element.26), channel_id=1, source_target_pairs={{0,12},{4,8},{8,4},{12,0},{1,13},{5,9},{9,5},{13,1},{2,14},{6,10},... | collective-permute-start | bytes 3145736 | tf_op jit(solution)/shard_map/ppermute | solution.py:22
  212.3 3.3 copy-start
  215.6 53.3 %all-to-all-start.1 = ((bf16[2048,4,256]{0,2,1:T(8,128)(2,1)}), bf16[2048,4,256]{0,2,1:T(8,128)(2,1)}, u32[]{:S(2)}, u32[]{:S(2)}) async-start(bf16[2048,4,256]{0,2,1:T(8,128)(2,1)} %bitcast.118), calls=%async_computation.1 | async-start | bytes 8388608 | tf_op jit(solution)/shard_map/all_to_all | solution.py:73
  222.7 6.9 %copy-start.1 = (bf16[2048,4,256]{0,2,1:T(8,128)(2,1)S(1)}, bf16[2048,4,256]{0,2,1:T(8,128)(2,1)}, u32[]{:S(2)}) copy-start(bf16[2048,4,256]{0,2,1:T(8,128)(2,1)} %copy-done) | copy-start | bytes 12582916
  230.7 8.4 %copy-start.3 = (bf16[2048,4,256]{0,2,1:T(8,128)(2,1)S(1)}, bf16[2048,4,256]{0,2,1:T(8,128)(2,1)}, u32[]{:S(2)}) copy-start(bf16[2048,4,256]{0,2,1:T(8,128)(2,1)} %broadcast_maximum_fusion.2) | copy-start | bytes 12582916
  268.8 53.1 %all-to-all-start.2 = ((bf16[2048,4,256]{0,2,1:T(8,128)(2,1)}), bf16[2048,4,256]{0,2,1:T(8,128)(2,1)}, u32[]{:S(2)}, u32[]{:S(2)}) async-start(bf16[2048,4,256]{0,2,1:T(8,128)(2,1)} %bitcast.124), calls=%async_computation.2 | async-start | bytes 8388608 | tf_op jit(solution)/shard_map/all_to_all | solution.py:73
  273.7 2.9 copy-start.11
  273.7 11.4 %slice-start = ((s8[16777216]{0:T(1024)(128)(4,1)}), s8[4194304]{0:T(1024)(128)(4,1)S(1)}, s32[]{:S(2)}) async-start(s8[16777216]{0:T(1024)(128)(4,1)} %bitcast.141), calls=%async_computation.5 | async-start | bytes 8388608
  276.6 8.5 %slice-start.1 = ((s8[16777216]{0:T(1024)(128)(4,1)}), s8[4194304]{0:T(1024)(128)(4,1)S(1)}, s32[]{:S(2)}) async-start(s8[16777216]{0:T(1024)(128)(4,1)} %bitcast.141), calls=%async_computation.6 | async-start | bytes 8388608
  276.6 8.5 %slice-start.2 = ((s8[16777216]{0:T(1024)(128)(4,1)}), s8[4194304]{0:T(1024)(128)(4,1)S(1)}, s32[]{:S(2)}) async-start(s8[16777216]{0:T(1024)(128)(4,1)} %bitcast.141), calls=%async_computation.7 | async-start | bytes 8388608
  276.6 8.6 %slice-start.3 = ((s8[16777216]{0:T(1024)(128)(4,1)}), s8[4194304]{0:T(1024)(128)(4,1)S(1)}, s32[]{:S(2)}) async-start(s8[16777216]{0:T(1024)(128)(4,1)} %bitcast.141), calls=%async_computation.8 | async-start | bytes 8388608
  285.1 6.1 %copy-start.4 = (bf16[2048,4,256]{0,2,1:T(8,128)(2,1)S(1)}, bf16[2048,4,256]{0,2,1:T(8,128)(2,1)}, u32[]{:S(2)}) copy-start(bf16[2048,4,256]{0,2,1:T(8,128)(2,1)} %broadcast_maximum_fusion.1) | copy-start | bytes 12582916
  321.9 55.6 %all-to-all-start.3 = ((bf16[2048,4,256]{0,2,1:T(8,128)(2,1)}), bf16[2048,4,256]{0,2,1:T(8,128)(2,1)}, u32[]{:S(2)}, u32[]{:S(2)}) async-start(bf16[2048,4,256]{0,2,1:T(8,128)(2,1)} %bitcast.122), calls=%async_computation.3 | async-start | bytes 8388608 | tf_op jit(solution)/shard_map/all_to_all | solution.py:73
  354.2 5.0 copy-start.12
  377.5 5.1 copy-start.8
  377.5 53.2 %all-to-all-start = ((bf16[2048,4,256]{0,2,1:T(8,128)(2,1)}), bf16[2048,4,256]{0,2,1:T(8,128)(2,1)}, u32[]{:S(2)}, u32[]{:S(2)}) async-start(bf16[2048,4,256]{0,2,1:T(8,128)(2,1)} %bitcast.123), calls=%async_computation | async-start | bytes 8388608 | tf_op jit(solution)/shard_map/all_to_all | solution.py:73
  382.5 169.5 %all-reduce.5.cloned.1.call-start = ((), (), s32[]{:S(2)}) async-start(), calls=%async_computation.4 | async-start | bytes 4194304
  382.6 17.3 %slice-start.8 = ((s8[16777216]{0:T(1024)(128)(4,1)}), s8[4194304]{0:T(1024)(128)(4,1)S(1)}, s32[]{:S(2)}) async-start(s8[16777216]{0:T(1024)(128)(4,1)} %bitcast.145), calls=%async_computation.13 | async-start | bytes 8388608
  382.6 17.3 %slice-start.9 = ((s8[16777216]{0:T(1024)(128)(4,1)}), s8[4194304]{0:T(1024)(128)(4,1)S(1)}, s32[]{:S(2)}) async-start(s8[16777216]{0:T(1024)(128)(4,1)} %bitcast.145), calls=%async_computation.14 | async-start | bytes 8388608
  391.4 8.5 %slice-start.10 = ((s8[16777216]{0:T(1024)(128)(4,1)}), s8[4194304]{0:T(1024)(128)(4,1)S(1)}, s32[]{:S(2)}) async-start(s8[16777216]{0:T(1024)(128)(4,1)} %bitcast.145), calls=%async_computation.15 | async-start | bytes 8388608
  391.4 8.5 %slice-start.11 = ((s8[16777216]{0:T(1024)(128)(4,1)}), s8[4194304]{0:T(1024)(128)(4,1)S(1)}, s32[]{:S(2)}) async-start(s8[16777216]{0:T(1024)(128)(4,1)} %bitcast.145), calls=%async_computation.16 | async-start | bytes 8388608
  430.8 8.8 %copy-start.19 = (f32[1024,1024]{1,0:T(8,128)S(1)}, f32[1024,1024]{1,0:T(8,128)}, u32[]{:S(2)}) copy-start(f32[1024,1024]{1,0:T(8,128)} %fusion.19) | copy-start | bytes 12582916
  430.8 8.8 %copy-start.20 = (f32[1024,1024]{1,0:T(8,128)S(1)}, f32[1024,1024]{1,0:T(8,128)}, u32[]{:S(2)}) copy-start(f32[1024,1024]{1,0:T(8,128)} %fusion.13) | copy-start | bytes 12582916
  430.8 8.8 %copy-start.21 = (f32[1024,1024]{1,0:T(8,128)S(1)}, f32[1024,1024]{1,0:T(8,128)}, u32[]{:S(2)}) copy-start(f32[1024,1024]{1,0:T(8,128)} %fusion.7) | copy-start | bytes 12582916
  464.5 7.6 %copy-start.5 = (bf16[2048,1024]{1,0:T(8,128)(2,1)S(1)}, bf16[2048,1024]{1,0:T(8,128)(2,1)}, u32[]{:S(2)}) copy-start(bf16[2048,1024]{1,0:T(8,128)(2,1)} %convolution_convert_fusion.4) | copy-start | bytes 12582916
  464.5 7.6 %copy-start.6 = (bf16[2048,1024]{1,0:T(8,128)(2,1)S(1)}, bf16[2048,1024]{1,0:T(8,128)(2,1)}, u32[]{:S(2)}) copy-start(bf16[2048,1024]{1,0:T(8,128)(2,1)} %convolution_convert_fusion.2) | copy-start | bytes 12582916
  464.5 7.6 %copy-start.7 = (bf16[2048,1024]{1,0:T(8,128)(2,1)S(1)}, bf16[2048,1024]{1,0:T(8,128)(2,1)}, u32[]{:S(2)}) copy-start(bf16[2048,1024]{1,0:T(8,128)(2,1)} %convolution_convert_fusion.6) | copy-start | bytes 12582916
  (3 other events, 5.6 us)
Sparse Core Ops, SparseCore 0:
  464.6 87.4 all-reduce.4
